TPU v7x, 256 devices: a whole 4x4x8 slice. The times are simulated.
256 devices in a mesh: dp: 4 (over z_hi), expert: 16 (over y, z_lo, core), mp: 4 (over x).
Axes of the slice: x: 4, y: 4, z: 8 (z_hi: 4, z_lo: 2; z = z_hi * 2 + z_lo), core: 2. Of those that a mesh axis runs over, the one named last changes fastest.
Arguments:
- hidden: bfloat16 [16384, 2048], P(('dp', 'expert', 'mp')), may hold values from -6 to 6
- norm_gain: float32 [2048], replicated, may hold values from 0.1 to 1.9
- expert_in: float32 [64, 2048, 2816], P('dp', ('expert', 'mp')), may hold values from -0.125 to 0.125
- expert_out: float32 [64, 2048, 1408], P('dp', ('expert', 'mp')), may hold values from -0.15625 to 0.15625
- expert_ids: int32 [16384, 6], P(('dp', 'expert', 'mp')), may hold values from 0 to 63, all different within a row; in each aligned block of 64 rows (0 to 63, 64 to 127, ...) at most 12 rows name the same one
- gate_levels: int32 [16384, 6], P(('dp', 'expert', 'mp')), may hold values from 1 to 255
- shared_gate: bfloat16 [2048, 2816], P(('dp', 'expert'), 'mp'), may hold values from -0.125 to 0.125
- shared_up: bfloat16 [2048, 2816], P(('dp', 'expert'), 'mp'), may hold values from -0.125 to 0.125
- shared_down: bfloat16 [2048, 2816], P(('dp', 'expert'), 'mp'), may hold values from -0.109375 to 0.109375
- next_gain: float32 [2048], replicated, may hold values from 0.1 to 1.9
- kv_weight: bfloat16 [2048, 576], P(None, 'mp'), may hold values from -0.125 to 0.125
Outputs:
- layer_out: bfloat16 [16384, 2048], P(('dp', 'expert', 'mp'))
- kv_latent: bfloat16 [16384, 576], P(('dp', 'expert'), 'mp')
Inputs may be any that keep to these rules, and one draw needn't show every extreme that they name: `expert_ids`: each row names 6 different experts. Among the 64 rows of one device no expert is named by more than 12 rows, and in every draw some expert is named by exactly 12 rows of some device.
All inputs are finite; a program needn't handle non-finite values.
Results may differ from a plain program's by a relative error of at most 0.012.
Values may be sent and summed in bfloat16 or wider, within the bound.
No kernel may reach another device: no remote copies, remote signals or barrier semaphores. Data moves between devices by JAX's collectives and lax.ppermute only.
A program may use at most 128 MiB of HBM per device.

v0:
```python
import jax
import jax.numpy as jnp
from jax import lax
from jax.sharding import PartitionSpec as P


def rms_scale(values, gain):
    wide = values.astype(jnp.float32)
    mean_sq = jnp.mean(wide * wide, axis=-1, keepdims=True)
    return (wide * lax.rsqrt(mean_sq + 1e-06) * gain).astype(jnp.bfloat16)


def expert_part(rows, gate_up_w, down_w):
    quarter = down_w.shape[1]
    gate_up = jnp.dot(rows, gate_up_w, preferred_element_type=jnp.float32)
    act = (jax.nn.silu(gate_up[:, :quarter]) * gate_up[:, quarter:]).astype(jnp.bfloat16)
    return lax.dot_general(
        act, down_w, (((1,), (1,)), ((), ())), preferred_element_type=jnp.float32
    )


def on_device(
    hidden,
    norm_gain,
    expert_in,
    expert_out,
    expert_ids,
    gate_levels,
    shared_gate,
    shared_up,
    shared_down,
    next_gain,
    kv_weight,
):
    tok_rows, width = hidden.shape
    top = expert_ids.shape[1]
    n_mp = lax.axis_size("mp")
    n_groups = lax.axis_size(("dp", "expert"))
    capacity = min(tok_rows, (2 * tok_rows * top + n_groups - 1) // n_groups)
    local_e, local_rows, double = expert_in.shape
    full_ff = double // 2
    quarter = full_ff // n_mp
    in_cast = (
        expert_in.astype(jnp.bfloat16)
        .reshape(local_e, local_rows, 2, n_mp, quarter)
        .transpose(0, 3, 1, 2, 4)
    )
    out_cast = (
        expert_out.astype(jnp.bfloat16)
        .reshape(local_e, local_rows, n_mp, quarter)
        .transpose(0, 2, 1, 3)
    )
    in_send = in_cast.reshape(local_e * n_mp, local_rows, 2, quarter)
    out_send = out_cast.reshape(local_e * n_mp, local_rows, quarter)
    in_recv, out_recv = (
        lax.all_to_all(in_send, ("expert", "mp"), split_axis=0, concat_axis=1, tiled=True),
        lax.all_to_all(out_send, ("expert", "mp"), split_axis=0, concat_axis=1, tiled=True),
    )
    gate_up_w = in_recv.reshape(width, 2 * quarter)
    down_w = out_recv.reshape(width, quarter)
    normed = rms_scale(hidden, norm_gain)
    levels = gate_levels.astype(jnp.float32)
    gate_weights = levels / jnp.sum(levels, axis=1, keepdims=True)
    flat_ids = expert_ids.reshape(-1)
    pairs = flat_ids.shape[0]
    onehot = (flat_ids[:, None] == jnp.arange(n_groups, dtype=jnp.int32)[None, :]).astype(jnp.int32)
    before = jnp.cumsum(onehot, axis=0) - onehot
    slot_of_pair = jnp.sum(before * onehot, axis=1)
    target = flat_ids * capacity + slot_of_pair
    token_of_pair = jnp.arange(pairs, dtype=jnp.int32) // top
    send = (
        jnp.zeros((n_groups * capacity, width), jnp.bfloat16).at[target].set(normed[token_of_pair])
    )
    received = lax.all_to_all(
        send.reshape(n_groups, capacity, width),
        ("dp", "expert"),
        split_axis=0,
        concat_axis=0,
        tiled=True,
    )
    slots_here = received.reshape(n_groups * capacity, width)
    every_slot = lax.all_gather(slots_here, "mp", axis=0, tiled=True)
    rows = every_slot
    summed = lax.psum_scatter(
        expert_part(rows, gate_up_w, down_w).astype(jnp.bfloat16),
        "mp",
        scatter_dimension=0,
        tiled=True,
    )
    result = summed.reshape(n_groups, capacity, width)
    back = lax.all_to_all(
        result, ("dp", "expert"), split_axis=0, concat_axis=0, tiled=True
    ).reshape(n_groups * capacity, width)
    picked = back[target].reshape(tok_rows, top, width)
    routed = jnp.sum(picked.astype(jnp.float32) * gate_weights[:, :, None], axis=1)
    gate_w, up_w, down_s = (
        lax.all_gather(shared_gate, ("dp", "expert"), axis=0, tiled=True),
        lax.all_gather(shared_up, ("dp", "expert"), axis=0, tiled=True),
        lax.all_gather(shared_down, ("dp", "expert"), axis=0, tiled=True),
    )
    group_rows = lax.all_gather(normed, "mp", axis=0, tiled=True)
    rows = group_rows
    gate_part = jnp.dot(rows, gate_w, preferred_element_type=jnp.float32)
    up_part = jnp.dot(rows, up_w, preferred_element_type=jnp.float32)
    act = (jax.nn.silu(gate_part) * up_part).astype(jnp.bfloat16)
    shared_out = lax.psum_scatter(
        lax.dot_general(act, down_s, (((1,), (1,)), ((), ())), preferred_element_type=jnp.float32),
        "mp",
        scatter_dimension=0,
        tiled=True,
    )
    layer_out = (hidden.astype(jnp.float32) + routed + shared_out).astype(jnp.bfloat16)
    next_rows = rms_scale(layer_out, next_gain)
    next_group = lax.all_gather(next_rows, "mp", axis=0, tiled=True)
    kv_latent = jnp.dot(next_group, kv_weight, preferred_element_type=jnp.float32).astype(
        jnp.bfloat16
    )
    return (layer_out, kv_latent)


def solution(mesh):
    in_specs = (
        P(("dp", "expert", "mp"), None),
        P(),
        P("dp", ("expert", "mp"), None),
        P("dp", ("expert", "mp"), None),
        P(("dp", "expert", "mp"), None),
        P(("dp", "expert", "mp"), None),
        P(("dp", "expert"), "mp"),
        P(("dp", "expert"), "mp"),
        P(("dp", "expert"), "mp"),
        P(),
        P(None, "mp"),
    )
    out_specs = (P(("dp", "expert", "mp"), None), P(("dp", "expert"), "mp"))
    return jax.shard_map(
        on_device, mesh=mesh, in_specs=in_specs, out_specs=out_specs, check_vma=False
    )
```

profile of v0, /device:TPU:1, one launch (start us, length us, event | category | flops | bytes accessed | tf_op | source)
XLA Modules:
  0.0 935.2 jit_solution(4523954897152339868)
XLA Ops:
  12.9 10.0 %scatter_custom_fusion = bf16[768,2048]{1,0:T(8,128)(2,1)} fusion(s32[384]{0:T(512)S(1)} %fusion.26, bf16[64,2048]{1,0:T(8,128)(2,1)S(1)} %fusion.18, s32[1024]{0:T(1024)S(1)} %pad_clamp_fusion.1, bf16[]{:T(256)} %constant.12.clone.1), kind=kCustom, calls=%fused_computation.9 | custom fusion | bytes 3145730 | tf_op jit(solution)/shard_map/scatter | solution.py:72
  22.8 6.1 reshape.153
  28.9 108.9 %all_to_all.28 = bf16[64,12,2048]{2,1,0:T(8,128)(2,1)} all-to-all(bf16[64,12,2048]{2,1,0:T(8,128)(2,1)} %reshape.153), channel_id=1, replica_groups=mesh['dp'=4,'expert'=16,'mp'=4] {'dp','expert'}, dimensions={0} | all-to-all | bytes 6291456 | tf_op jit(solution)/shard_map/all_to_all | solution.py:74
  137.8 6.2 reshape.154
  147.0 5.1 reshape.155
  156.9 9.3 all-to-all-start.1
  168.2 54.8 %all-to-all-done.1 = bf16[64,32,2,352]{3,1,2,0:T(8,128)(2,1)} async-done(((bf16[64,32,2,352]{3,1,2,0:T(8,128)(2,1)}), bf16[64,32,2,352]{3,1,2,0:T(8,128)(2,1)}, u32[]{:S(2)}, u32[]{:S(2)}) %all-to-all-start.1) | async-done | bytes 2883616 | tf_op jit(solution)/shard_map/all_to_all | solution.py:56
  227.5 6.9 copy.25
  234.4 7.8 reshape.157
  242.2 70.8 %all-gather.7.cloned.1.call-done = bf16[3072,2048]{1,0:T(8,128)(2,1)} async-done(((bf16[768,2048]{1,0:T(8,128)(2,1)}), bf16[3072,2048]{1,0:T(8,128)(2,1)}) %all-gather.7.cloned.1.call-update) | async-done | bytes 12582928 | tf_op jit(solution)/shard_map/all_gather | solution.py:82
  313.0 15.2 %fusion.32 = f32[3072,704]{0,1:T(8,128)} fusion(bf16[3072,2048]{1,0:T(8,128)(2,1)} %all-gather.7.cloned.1.call-done, bf16[2048,704]{1,0:T(8,128)(2,1)} %reshape.157), kind=kOutput, calls=%fused_computation.62 | convolution fusion | flops 8858370048 | bytes 24117248 | tf_op jit(solution)/shard_map/dot_general | solution.py:15
  328.1 13.5 %convolution_convert_fusion = bf16[3072,2048]{1,0:T(8,128)(2,1)} fusion(bf16[2048,352]{1,0:T(8,128)(2,1)S(1)} %bitcast.36, f32[3072,704]{0,1:T(8,128)} %fusion.32), kind=kOutput, calls=%fused_computation.3 | convolution fusion | flops 4441964544 | bytes 22675456 | tf_op jit(solution)/shard_map/dot_general | solution.py:17
  344.1 115.7 %reduce-scatter.3.cloned.1.call-done = bf16[768,2048]{1,0:T(8,128)(2,1)} async-done(((bf16[3072,2048]{1,0:T(8,128)(2,1)}), bf16[768,2048]{1,0:T(8,128)(2,1)}) %reduce-scatter.3.cloned.1.call-update) | async-done | bytes 3145744 | tf_op jit(solution)/shard_map/reduce_scatter | solution.py:84
  459.8 6.1 reshape.160
  465.9 10.8 %all-to-all-start.3 = ((bf16[64,12,2048]{2,1,0:T(8,128)(2,1)}), bf16[64,12,2048]{2,1,0:T(8,128)(2,1)}, u32[]{:S(2)}, u32[]{:S(2)}) async-start(bf16[64,12,2048]{2,1,0:T(8,128)(2,1)} %reshape.160), calls=%async_computation.4 | async-start | bytes 8388608 | tf_op jit(solution)/shard_map/all_to_all | solution.py:91
  477.0 10.5 %all-gather.9.cloned.1.call-done = bf16[256,2048]{1,0:T(8,128)(2,1)} async-done(((bf16[64,2048]{1,0:T(8,128)(2,1)}), bf16[256,2048]{1,0:T(8,128)(2,1)}) %all-gather.9.cloned.1.call-update) | async-done | bytes 1048592 | tf_op jit(solution)/shard_map/all_gather | solution.py:101
  487.6 139.0 %all-gather.11.cloned.1.call-done = bf16[2048,704]{1,0:T(8,128)(2,1)} async-done(((bf16[32,704]{1,0:T(8,128)(2,1)}), bf16[2048,704]{1,0:T(8,128)(2,1)}) %all-gather.11.cloned.1.call-update) | async-done | bytes 2883600 | tf_op jit(solution)/shard_map/all_gather | solution.py:97
  630.1 114.3 %all-gather.13.cloned.1.call-done = bf16[2048,704]{1,0:T(8,128)(2,1)} async-done(((bf16[32,704]{1,0:T(8,128)(2,1)}), bf16[2048,704]{1,0:T(8,128)(2,1)}) %all-gather.13.cloned.1.call-update) | async-done | bytes 2883600 | tf_op jit(solution)/shard_map/all_gather | solution.py:98
  744.4 115.5 %all-gather.15.cloned.1.call-done = bf16[2048,704]{1,0:T(8,128)(2,1)} async-done(((bf16[32,704]{1,0:T(8,128)(2,1)}), bf16[2048,704]{1,0:T(8,128)(2,1)}) %all-gather.15.cloned.1.call-update) | async-done | bytes 2883600 | tf_op jit(solution)/shard_map/all_gather | solution.py:99
  860.0 7.6 fusion.7
  867.8 6.2 reshape.161
  874.0 6.7 gather_fusion
  886.7 11.5 %reduce-scatter.5.cloned.1.call-done = f32[64,2048]{1,0:T(8,128)} async-done(((f32[256,2048]{1,0:T(8,128)}), f32[64,2048]{1,0:T(8,128)}) %reduce-scatter.5.cloned.1.call-update) | async-done | bytes 524304 | tf_op jit(solution)/shard_map/reduce_scatter | solution.py:106
  900.3 25.5 %all-gather.17.cloned.1.call-done = bf16[256,2048]{1,0:T(8,128)(2,1)} async-done(((bf16[64,2048]{1,0:T(8,128)(2,1)}), bf16[256,2048]{1,0:T(8,128)(2,1)}) %all-gather.17.cloned.1.call-update) | async-done | bytes 1048592 | tf_op jit(solution)/shard_map/all_gather | solution.py:114
  (68 shorter events, 36.7 us)
Async XLA Ops:
  7.2 918.6 %copy-start = (bf16[2048,144]{0,1:T(8,128)(2,1)S(1)}, bf16[2048,144]{0,1:T(8,128)(2,1)}, u32[]{:S(2)}) copy-start(bf16[2048,144]{0,1:T(8,128)(2,1)} %param.21) | copy-start | bytes 1769476
  7.2 305.8 %all-gather.7.cloned.1.call-start = ((), (), s32[]{:S(2)}) async-start(), calls=%async_computation.6 | async-start | bytes 15728640 | tf_op jit(solution)/shard_map/all_gather | solution.py:82
  12.9 16.1 %copy-start.3 = (bf16[64,2048]{1,0:T(8,128)(2,1)}, bf16[64,2048]{1,0:T(8,128)(2,1)S(1)}, u32[]{:S(2)}) copy-start(bf16[64,2048]{1,0:T(8,128)(2,1)S(1)} %fusion.18) | copy-start | bytes 786436
  156.9 9.3 copy-start.1
  156.9 66.2 %all-to-all-start.1 = ((bf16[64,32,2,352]{3,1,2,0:T(8,128)(2,1)}), bf16[64,32,2,352]{3,1,2,0:T(8,128)(2,1)}, u32[]{:S(2)}, u32[]{:S(2)}) async-start(bf16[64,32,2,352]{3,1,2,0:T(8,128)(2,1)} %bitcast.34), calls=%async_computation.1 | async-start | bytes 6291456 | tf_op jit(solution)/shard_map/all_to_all | solution.py:56
  223.1 105.1 %all-to-all-start.2 = ((bf16[64,32,352]{2,1,0:T(8,128)(2,1)}), bf16[64,32,352]{2,1,0:T(8,128)(2,1)S(1)}, u32[]{:S(2)}, u32[]{:S(2)}) async-start(bf16[64,32,352]{2,1,0:T(8,128)(2,1)} %bitcast.3), calls=%async_computation.2 | async-start | bytes 3145728 | tf_op jit(solution)/shard_map/all_to_all | solution.py:57
  227.4 232.4 %reduce-scatter.3.cloned.1.call-start = ((), (), s32[]{:S(2)}) async-start(), calls=%async_computation.7 | async-start | bytes 15728640 | tf_op jit(solution)/shard_map/reduce_scatter | solution.py:84
  341.6 146.0 %all-gather.9.cloned.1.call-start = ((), (), s32[]{:S(2)}) async-start(), calls=%async_computation.8 | async-start | bytes 1310720 | tf_op jit(solution)/shard_map/all_gather | solution.py:101
  342.3 284.3 %all-gather.11.cloned.1.call-start = ((), (), s32[]{:S(2)}) async-start(), calls=%async_computation.9 | async-start | bytes 3194880 | tf_op jit(solution)/shard_map/all_gather | solution.py:97
  342.9 401.5 %all-gather.13.cloned.1.call-start = ((), (), s32[]{:S(2)}) async-start(), calls=%async_computation.10 | async-start | bytes 3194880 | tf_op jit(solution)/shard_map/all_gather | solution.py:98
  343.5 516.4 %all-gather.15.cloned.1.call-start = ((), (), s32[]{:S(2)}) async-start(), calls=%async_computation.11 | async-start | bytes 3194880 | tf_op jit(solution)/shard_map/all_gather | solution.py:99
  465.9 401.9 %all-to-all-start.3 = ((bf16[64,12,2048]{2,1,0:T(8,128)(2,1)}), bf16[64,12,2048]{2,1,0:T(8,128)(2,1)}, u32[]{:S(2)}, u32[]{:S(2)}) async-start(bf16[64,12,2048]{2,1,0:T(8,128)(2,1)} %reshape.160), calls=%async_computation.4 | async-start | bytes 8388608 | tf_op jit(solution)/shard_map/all_to_all | solution.py:91
  476.8 421.4 %reduce-scatter.5.cloned.1.call-start = ((), (), s32[]{:S(2)}) async-start(), calls=%async_computation.12 | async-start | bytes 2621440 | tf_op jit(solution)/shard_map/reduce_scatter | solution.py:106
  487.6 372.4 %copy-start.7 = (bf16[256,2048]{1,0:T(8,128)(2,1)S(1)}, bf16[256,2048]{1,0:T(8,128)(2,1)}, u32[]{:S(2)}) copy-start(bf16[256,2048]{1,0:T(8,128)(2,1)} %all-gather.9.cloned.1.call-done) | copy-start | bytes 3145732
  630.1 237.5 %copy-start.5 = (s32[64,6]{0,1:T(8,128)S(1)}, s32[64,6]{0,1:T(8,128)}, u32[]{:S(2)}) copy-start(s32[64,6]{0,1:T(8,128)} %param.16) | copy-start | bytes 4612
  867.6 58.2 %all-gather.17.cloned.1.call-start = ((), (), s32[]{:S(2)}) async-start(), calls=%async_computation.13 | async-start | bytes 1310720 | tf_op jit(solution)/shard_map/all_gather | solution.py:114
  882.8 15.3 %copy-start.2 = (bf16[64,2048]{1,0:T(8,128)(2,1)S(1)}, bf16[64,2048]{1,0:T(8,128)(2,1)}, u32[]{:S(2)}) copy-start(bf16[64,2048]{1,0:T(8,128)(2,1)} %param.11) | copy-start | bytes 786436
  882.8 16.6 %copy-start.6 = (f32[2048]{0:T(1024)S(1)}, f32[2048]{0:T(1024)}, u32[]{:S(2)}) copy-start(f32[2048]{0:T(1024)} %param.20) | copy-start | bytes 24580
  899.4 28.7 %copy-start.4 = (bf16[64,2048]{1,0:T(8,128)(2,1)}, bf16[64,2048]{1,0:T(8,128)(2,1)S(1)}, u32[]{:S(2)}) copy-start(bf16[64,2048]{1,0:T(8,128)(2,1)S(1)} %get-tuple-element.3) | copy-start | bytes 786436
Sparse Core Ops, SparseCore 0:
  144.1 168.7 all-gather.6
  341.7 118.0 reduce-scatter.2
  462.2 25.2 all-gather.8
  489.3 137.2 all-gather.10
  628.3 116.0 all-gather.12
  746.1 113.7 all-gather.14
  867.7 30.4 reduce-scatter.4
  900.4 25.2 all-gather.16
where the time goes:
time: 945 us; the launch traced here: 935 us
  waiting for transfers between devices  660 us (70%)
  blocking collectives  109 us (12%)
  local copies, waits for them, and re-layouts  70.1 us (7%)
  matrix products  42.1 us (4%)
  starting transfers between devices  25.1 us (3%)
  between operations  14.6 us (2%)
  other arithmetic  14.5 us (2%)
    all_gather x1, waiting for transfers between devices, on_device(): lax.all_gather(shared_gate, ('dp', 'expert'), axis=0, tiled=True)  139 us
    reduce_scatter x1, waiting for transfers between devices, on_device(): lax.psum_scatter(expert_part(rows, gate_up_w, down_w).astype(jnp.bfloat16...  116 us
    all_gather x1, waiting for transfers between devices, on_device(): lax.all_gather(shared_down, ('dp', 'expert'), axis=0, tiled=True)  116 us
    all_gather x1, waiting for transfers between devices, on_device(): lax.all_gather(shared_up, ('dp', 'expert'), axis=0, tiled=True)  114 us
    all_to_all x1, blocking collectives, on_device(): lax.all_to_all(send.reshape(n_groups, capacity, width), ('dp', 'expert'),...  109 us
    all_gather x1, waiting for transfers between devices, on_device(): every_slot = lax.all_gather(slots_here, 'mp', axis=0, tiled=True)  70.8 us
    all_to_all x1, waiting for transfers between devices, on_device(): lax.all_to_all(in_send, ('expert', 'mp'), split_axis=0, concat_axis=1, ti...  54.8 us
    all_gather x1, waiting for transfers between devices, on_device(): next_group = lax.all_gather(next_rows, 'mp', axis=0, tiled=True)  25.5 us
  transfers between devices with their start and end apart: 11, of which 9 were waited for; matrix products, arithmetic and copies ran while one was open for 9% of the time, Pallas kernels for 0%

commit v1 on v0

--- a/solution.py
+++ b/solution.py
@@ -2,6 +2,14 @@
 import jax.numpy as jnp
 from jax import lax
 from jax.sharding import PartitionSpec as P
+
+
+def rates_play(inp):
+    inter = lax.axis_size(("expert", "mp"))
+    aux = jnp.stack(jnp.split(inp, inter, axis=0), axis=0)
+    parts_out = lax.all_to_all(aux, ("expert", "mp"), 0, 0)
+    block_next = jnp.concatenate(parts_out, axis=1)
+    return block_next
 
 
 def rms_scale(values, gain):
@@ -53,7 +61,7 @@
     in_send = in_cast.reshape(local_e * n_mp, local_rows, 2, quarter)
     out_send = out_cast.reshape(local_e * n_mp, local_rows, quarter)
     in_recv, out_recv = (
-        lax.all_to_all(in_send, ("expert", "mp"), split_axis=0, concat_axis=1, tiled=True),
+        rates_play(in_send),
         lax.all_to_all(out_send, ("expert", "mp"), split_axis=0, concat_axis=1, tiled=True),
     )
     gate_up_w = in_recv.reshape(width, 2 * quarter)

time: 945 us -> 946 us (level)
  blocking collectives: 109 us -> 0 us
  local copies, waits for them, and re-layouts: 70.1 us -> 152 us
  starting transfers between devices: 25.1 us -> 40 us
  waiting for transfers between devices: 660 us -> 670 us
    all_to_all x1 -> x0, blocking collectives: 109 us -> none  [on_device(): lax.all_to_all(send.reshape(n_groups, capacity, width), ('dp', 'expert'),...]
    unnamed x17 -> x82, local copies, waits for them, and re-layouts: 0.87 us -> 83.5 us
    all_to_all x1 -> x2, waiting for transfers between devices: 54.8 us -> 132 us  [the longest x1 76.8 us: on_device(): lax.all_to_all(send.reshape(n_groups, capacity, width), ('dp', 'expert'),...]
    all_gather x1, waiting for transfers between devices: 70.8 us -> 0.01 us  [on_device(): every_slot = lax.all_gather(slots_here, 'mp', axis=0, tiled=True)]
    all_to_all x1 -> x2, starting transfers between devices: 9.32 us -> 23.8 us  [the longest x1 13.3 us: on_device(): lax.all_to_all(send.reshape(n_groups, capacity, width), ('dp', 'expert'),...]
  transfers between devices with their start and end apart: 11 -> 12, of which waited for: 9 -> 9; matrix products, arithmetic and copies ran while one was open for 9% -> 17% of each run, Pallas kernels for 0% -> 0%
where the time goes in v1:
time: 946 us; the launch traced here: 933 us
  waiting for transfers between devices  670 us (71%)
  local copies, waits for them, and re-layouts  152 us (16%)
  matrix products  42.1 us (4%)
  starting transfers between devices  40 us (4%)
  between operations  14.6 us (2%)
  other arithmetic  14.5 us (2%)
    all_gather x1, waiting for transfers between devices, on_device(): lax.all_gather(shared_gate, ('dp', 'expert'), axis=0, tiled=True)  139 us
    reduce_scatter x1, waiting for transfers between devices, on_device(): lax.psum_scatter(expert_part(rows, gate_up_w, down_w).astype(jnp.bfloat16...  120 us
    all_gather x1, waiting for transfers between devices, on_device(): lax.all_gather(shared_down, ('dp', 'expert'), axis=0, tiled=True)  116 us
    all_gather x1, waiting for transfers between devices, on_device(): lax.all_gather(shared_up, ('dp', 'expert'), axis=0, tiled=True)  114 us
    unnamed x82, local copies, waits for them, and re-layouts  83.5 us
    all_to_all x1, waiting for transfers between devices, on_device(): lax.all_to_all(send.reshape(n_groups, capacity, width), ('dp', 'expert'),...  76.8 us
    all_to_all x1, waiting for transfers between devices, rates_play(): parts_out = lax.all_to_all(aux, ('expert', 'mp'), 0, 0)  54.8 us
    all_gather x1, waiting for transfers between devices, on_device(): next_group = lax.all_gather(next_rows, 'mp', axis=0, tiled=True)  25.5 us
  transfers between devices with their start and end apart: 12, of which 9 were waited for; matrix products, arithmetic and copies ran while one was open for 17% of the time, Pallas kernels for 0%

profile of v1, /device:TPU:1, one launch (start us, length us, event | category | flops | bytes accessed | tf_op | source)
XLA Modules:
  0.0 933.1 jit_solution(978506361413794132)
XLA Ops:
  12.8 9.9 %scatter_custom_fusion = bf16[768,2048]{1,0:T(8,128)(2,1)} fusion(s32[384]{0:T(512)S(1)} %fusion.26, bf16[64,2048]{1,0:T(8,128)(2,1)S(1)} %fusion.18, s32[1024]{0:T(1024)S(1)} %pad_clamp_fusion.1, bf16[]{:T(256)} %constant.12.clone.1), kind=kCustom, calls=%fused_computation.9 | custom fusion | bytes 3145730 | tf_op jit(solution)/shard_map/scatter | solution.py:80
  22.8 6.1 reshape.146
  28.9 13.3 %all-to-all-start = ((bf16[64,12,2048]{2,1,0:T(8,128)(2,1)}), bf16[64,12,2048]{2,1,0:T(8,128)(2,1)}, u32[]{:S(2)}, u32[]{:S(2)}) async-start(bf16[64,12,2048]{2,1,0:T(8,128)(2,1)} %reshape.146), calls=%async_computation | async-start | bytes 8388608 | tf_op jit(solution)/shard_map/all_to_all | solution.py:82
  45.8 5.0 reshape.148
  59.5 76.8 %all-to-all-done = bf16[64,12,2048]{2,1,0:T(8,128)(2,1)} async-done(((bf16[64,12,2048]{2,1,0:T(8,128)(2,1)}), bf16[64,12,2048]{2,1,0:T(8,128)(2,1)}, u32[]{:S(2)}, u32[]{:S(2)}) %all-to-all-start) | async-done | bytes 3145760 | tf_op jit(solution)/shard_map/all_to_all | solution.py:82
  136.3 6.1 reshape.147
  220.5 10.4 %all-to-all-start.1 = ((bf16[64,1,32,2,352]{4,2,3,1,0:T(8,128)(2,1)}), bf16[64,1,32,2,352]{4,2,3,1,0:T(8,128)(2,1)}, u32[]{:S(2)}, u32[]{:S(2)}) async-start(bf16[64,1,32,2,352]{4,2,3,1,0:T(8,128)(2,1)} %constant_dynamic-update-slice_fusion), calls=%async_computation.1 | async-start | bytes 6291456 | tf_op jit(solution)/shard_map/all_to_all | solution.py:10
  232.9 54.8 %all-to-all-done.1 = bf16[64,1,32,2,352]{4,2,3,1,0:T(8,128)(2,1)} async-done(((bf16[64,1,32,2,352]{4,2,3,1,0:T(8,128)(2,1)}), bf16[64,1,32,2,352]{4,2,3,1,0:T(8,128)(2,1)}, u32[]{:S(2)}, u32[]{:S(2)}) %all-to-all-start.1) | async-done | bytes 2883616 | tf_op jit(solution)/shard_map/all_to_all | solution.py:10
  292.2 6.9 copy.25
  299.1 7.8 reshape_reshape.3
  306.9 15.2 %fusion.32 = f32[3072,704]{0,1:T(8,128)} fusion(bf16[3072,2048]{1,0:T(8,128)(2,1)} %all-gather.7.cloned.1.call-done, bf16[2048,704]{1,0:T(8,128)(2,1)} %reshape_reshape.3), kind=kOutput, calls=%fused_computation.190 | convolution fusion | flops 8858370048 | bytes 24117248 | tf_op jit(solution)/shard_map/dot_general | solution.py:23
  322.1 13.5 %convolution_convert_fusion = bf16[3072,2048]{1,0:T(8,128)(2,1)} fusion(bf16[2048,352]{1,0:T(8,128)(2,1)S(1)} %bitcast.357, f32[3072,704]{0,1:T(8,128)} %fusion.32), kind=kOutput, calls=%fused_computation.3 | convolution fusion | flops 4441964544 | bytes 22675456 | tf_op jit(solution)/shard_map/dot_general | solution.py:25
  338.0 120.1 %reduce-scatter.3.cloned.1.call-done = bf16[768,2048]{1,0:T(8,128)(2,1)} async-done(((bf16[3072,2048]{1,0:T(8,128)(2,1)}), bf16[768,2048]{1,0:T(8,128)(2,1)}) %reduce-scatter.3.cloned.1.call-update) | async-done | bytes 3145744 | tf_op jit(solution)/shard_map/reduce_scatter | solution.py:92
  458.1 6.1 reshape.152
  464.3 10.8 %all-to-all-start.3 = ((bf16[64,12,2048]{2,1,0:T(8,128)(2,1)}), bf16[64,12,2048]{2,1,0:T(8,128)(2,1)}, u32[]{:S(2)}, u32[]{:S(2)}) async-start(bf16[64,12,2048]{2,1,0:T(8,128)(2,1)} %reshape.152), calls=%async_computation.4 | async-start | bytes 8388608 | tf_op jit(solution)/shard_map/all_to_all | solution.py:99
  475.4 10.5 %all-gather.9.cloned.1.call-done = bf16[256,2048]{1,0:T(8,128)(2,1)} async-done(((bf16[64,2048]{1,0:T(8,128)(2,1)}), bf16[256,2048]{1,0:T(8,128)(2,1)}) %all-gather.9.cloned.1.call-update) | async-done | bytes 1048592 | tf_op jit(solution)/shard_map/all_gather | solution.py:109
  485.9 138.9 %all-gather.11.cloned.1.call-done = bf16[2048,704]{1,0:T(8,128)(2,1)} async-done(((bf16[32,704]{1,0:T(8,128)(2,1)}), bf16[2048,704]{1,0:T(8,128)(2,1)}) %all-gather.11.cloned.1.call-update) | async-done | bytes 2883600 | tf_op jit(solution)/shard_map/all_gather | solution.py:105
  628.4 114.0 %all-gather.13.cloned.1.call-done = bf16[2048,704]{1,0:T(8,128)(2,1)} async-done(((bf16[32,704]{1,0:T(8,128)(2,1)}), bf16[2048,704]{1,0:T(8,128)(2,1)}) %all-gather.13.cloned.1.call-update) | async-done | bytes 2883600 | tf_op jit(solution)/shard_map/all_gather | solution.py:106
  742.3 115.5 %all-gather.15.cloned.1.call-done = bf16[2048,704]{1,0:T(8,128)(2,1)} async-done(((bf16[32,704]{1,0:T(8,128)(2,1)}), bf16[2048,704]{1,0:T(8,128)(2,1)}) %all-gather.15.cloned.1.call-update) | async-done | bytes 2883600 | tf_op jit(solution)/shard_map/all_gather | solution.py:107
  857.9 7.6 fusion.7
  865.7 6.2 reshape.153
  871.9 6.7 gather_fusion
  884.6 11.5 %reduce-scatter.5.cloned.1.call-done = f32[64,2048]{1,0:T(8,128)} async-done(((f32[256,2048]{1,0:T(8,128)}), f32[64,2048]{1,0:T(8,128)}) %reduce-scatter.5.cloned.1.call-update) | async-done | bytes 524304 | tf_op jit(solution)/shard_map/reduce_scatter | solution.py:114
  898.2 25.5 %all-gather.17.cloned.1.call-done = bf16[256,2048]{1,0:T(8,128)(2,1)} async-done(((bf16[64,2048]{1,0:T(8,128)(2,1)}), bf16[256,2048]{1,0:T(8,128)(2,1)}) %all-gather.17.cloned.1.call-update) | async-done | bytes 1048592 | tf_op jit(solution)/shard_map/all_gather | solution.py:122
  (135 shorter events, 119.1 us)
Async XLA Ops:
  7.2 916.5 %copy-start = (bf16[2048,144]{0,1:T(8,128)(2,1)S(1)}, bf16[2048,144]{0,1:T(8,128)(2,1)}, u32[]{:S(2)}) copy-start(bf16[2048,144]{0,1:T(8,128)(2,1)} %param.21) | copy-start | bytes 1769476
  12.8 16.1 %copy-start.4 = (bf16[64,2048]{1,0:T(8,128)(2,1)}, bf16[64,2048]{1,0:T(8,128)(2,1)S(1)}, u32[]{:S(2)}) copy-start(bf16[64,2048]{1,0:T(8,128)(2,1)S(1)} %fusion.18) | copy-start | bytes 786436
  28.9 107.4 %all-to-all-start = ((bf16[64,12,2048]{2,1,0:T(8,128)(2,1)}), bf16[64,12,2048]{2,1,0:T(8,128)(2,1)}, u32[]{:S(2)}, u32[]{:S(2)}) async-start(bf16[64,12,2048]{2,1,0:T(8,128)(2,1)} %reshape.146), calls=%async_computation | async-start | bytes 8388608 | tf_op jit(solution)/shard_map/all_to_all | solution.py:82
  42.2 264.7 %all-gather.7.cloned.1.call-start = ((), (), s32[]{:S(2)}) async-start(), calls=%async_computation.6 | async-start | bytes 15728640 | tf_op jit(solution)/shard_map/all_gather | solution.py:90
  53.4 5.4 copy-start.1
  220.5 10.5 %copy-start.2 = (f32[16,32,1408]{2,1,0:T(8,128)S(1)}, f32[16,32,1408]{2,1,0:T(8,128)}, u32[]{:S(2)}) copy-start(f32[16,32,1408]{2,1,0:T(8,128)} %param.14) | copy-start | bytes 8650756
  220.5 67.3 %all-to-all-start.1 = ((bf16[64,1,32,2,352]{4,2,3,1,0:T(8,128)(2,1)}), bf16[64,1,32,2,352]{4,2,3,1,0:T(8,128)(2,1)}, u32[]{:S(2)}, u32[]{:S(2)}) async-start(bf16[64,1,32,2,352]{4,2,3,1,0:T(8,128)(2,1)} %constant_dynamic-update-slice_fusion), calls=%async_computation.1 | async-start | bytes 6291456 | tf_op jit(solution)/shard_map/all_to_all | solution.py:10
  287.8 34.3 %all-to-all-start.2 = ((bf16[64,32,352]{2,1,0:T(8,128)(2,1)}), bf16[64,32,352]{2,1,0:T(8,128)(2,1)S(1)}, u32[]{:S(2)}, u32[]{:S(2)}) async-start(bf16[64,32,352]{2,1,0:T(8,128)(2,1)} %bitcast.67), calls=%async_computation.2 | async-start | bytes 3145728 | tf_op jit(solution)/shard_map/all_to_all | solution.py:65
  292.2 166.0 %reduce-scatter.3.cloned.1.call-start = ((), (), s32[]{:S(2)}) async-start(), calls=%async_computation.7 | async-start | bytes 15728640 | tf_op jit(solution)/shard_map/reduce_scatter | solution.py:92
  335.6 150.3 %all-gather.9.cloned.1.call-start = ((), (), s32[]{:S(2)}) async-start(), calls=%async_computation.8 | async-start | bytes 1310720 | tf_op jit(solution)/shard_map/all_gather | solution.py:109
  336.3 288.5 %all-gather.11.cloned.1.call-start = ((), (), s32[]{:S(2)}) async-start(), calls=%async_computation.9 | async-start | bytes 3194880 | tf_op jit(solution)/shard_map/all_gather | solution.py:105
  336.9 405.5 %all-gather.13.cloned.1.call-start = ((), (), s32[]{:S(2)}) async-start(), calls=%async_computation.10 | async-start | bytes 3194880 | tf_op jit(solution)/shard_map/all_gather | solution.py:106
  337.5 520.4 %all-gather.15.cloned.1.call-start = ((), (), s32[]{:S(2)}) async-start(), calls=%async_computation.11 | async-start | bytes 3194880 | tf_op jit(solution)/shard_map/all_gather | solution.py:107
  464.3 401.5 %all-to-all-start.3 = ((bf16[64,12,2048]{2,1,0:T(8,128)(2,1)}), bf16[64,12,2048]{2,1,0:T(8,128)(2,1)}, u32[]{:S(2)}, u32[]{:S(2)}) async-start(bf16[64,12,2048]{2,1,0:T(8,128)(2,1)} %reshape.152), calls=%async_computation.4 | async-start | bytes 8388608 | tf_op jit(solution)/shard_map/all_to_all | solution.py:99
  475.1 421.0 %reduce-scatter.5.cloned.1.call-start = ((), (), s32[]{:S(2)}) async-start(), calls=%async_computation.12 | async-start | bytes 2621440 | tf_op jit(solution)/shard_map/reduce_scatter | solution.py:114
  485.9 372.0 %copy-start.8 = (bf16[256,2048]{1,0:T(8,128)(2,1)S(1)}, bf16[256,2048]{1,0:T(8,128)(2,1)}, u32[]{:S(2)}) copy-start(bf16[256,2048]{1,0:T(8,128)(2,1)} %all-gather.9.cloned.1.call-done) | copy-start | bytes 3145732
  628.4 237.2 %copy-start.6 = (s32[64,6]{0,1:T(8,128)S(1)}, s32[64,6]{0,1:T(8,128)}, u32[]{:S(2)}) copy-start(s32[64,6]{0,1:T(8,128)} %param.16) | copy-start | bytes 4612
  865.5 58.2 %all-gather.17.cloned.1.call-start = ((), (), s32[]{:S(2)}) async-start(), calls=%async_computation.13 | async-start | bytes 1310720 | tf_op jit(solution)/shard_map/all_gather | solution.py:122
  880.8 15.3 %copy-start.3 = (bf16[64,2048]{1,0:T(8,128)(2,1)S(1)}, bf16[64,2048]{1,0:T(8,128)(2,1)}, u32[]{:S(2)}) copy-start(bf16[64,2048]{1,0:T(8,128)(2,1)} %param.11) | copy-start | bytes 786436
  880.8 16.6 %copy-start.7 = (f32[2048]{0:T(1024)S(1)}, f32[2048]{0:T(1024)}, u32[]{:S(2)}) copy-start(f32[2048]{0:T(1024)} %param.20) | copy-start | bytes 24580
  897.3 28.7 %copy-start.5 = (bf16[64,2048]{1,0:T(8,128)(2,1)}, bf16[64,2048]{1,0:T(8,128)(2,1)S(1)}, u32[]{:S(2)}) copy-start(bf16[64,2048]{1,0:T(8,128)(2,1)S(1)} %get-tuple-element.3) | copy-start | bytes 786436
Sparse Core Ops, SparseCore 0:
  142.5 153.7 all-gather.6
  335.7 122.3 reduce-scatter.2
  460.5 25.3 all-gather.8
  487.6 137.1 all-gather.10
  626.5 115.7 all-gather.12
  744.1 113.7 all-gather.14
  865.6 30.4 reduce-scatter.4
  898.3 25.2 all-gather.16
